TPU v7x, 512 devices: a whole 4x8x8 slice. The times are simulated.
512 devices in a mesh: section: 32 (over z, x), neuron: 16 (over y, core).
Axes of the slice: x: 4, y: 8, z: 8, core: 2. Of those that a mesh axis runs over, the one named last changes fastest.
Arguments:
- inputs: bfloat16 [6, 32768], P(None, 'neuron'), may hold values from 0 to 2
- weight_tiles: bfloat16 [32, 2048, 128, 128], P('section', 'neuron'), may hold values from -0.07324219 to 0.07910156
- source_block: int32 [32, 2048], P('section', 'neuron'), may hold values from 0 to 255
- target_block: int32 [32, 2048], P('section', 'neuron'), may hold values from 0 to 15
- live_slots: int32 [32, 16], P('section', 'neuron'), may hold values from 16 to 128, as said below
Outputs:
- activations: bfloat16 [32, 6, 32768], P('section', None, 'neuron')
Inputs may be any that keep to these rules, and one draw needn't show every extreme that they name: live_slots[l, n] is 128, 64, 32 or 16, and in every layer some shard has all 128 slots live.
All inputs are finite; a program needn't handle non-finite values.
Results may differ from a plain program's by a relative error of at most 0.0045.
Values may be sent and summed in bfloat16 or wider, within the bound.
No kernel may reach another device: no remote copies, remote signals or barrier semaphores. Data moves between devices by JAX's collectives and lax.ppermute only.
A program may use at most 64 MiB of HBM per device.

v0:
```python
import jax
import jax.numpy as jnp
from jax import lax
from jax.sharding import PartitionSpec as P

NEURON_BIAS = -0.3
CLIP_LEVEL = 32.0
UNROLL = True


def layer_apply(gathered, weight_tiles, source, selector):
    row_count = gathered.shape[0]
    block_size = weight_tiles.shape[2]
    column_count = selector.shape[1]
    block_count = gathered.shape[1] // block_size
    shaped = gathered.reshape(row_count, block_count, block_size)
    picked = shaped.at[:, source].get(mode="promise_in_bounds")
    partial_value = jnp.einsum(
        "msk,skj->msj", picked, weight_tiles[0], preferred_element_type=jnp.float32
    )
    summed = jnp.einsum("msj,sc->mcj", partial_value, selector, precision=lax.Precision.HIGHEST)
    result = jnp.clip(summed + NEURON_BIAS, 0.0, CLIP_LEVEL).astype(jnp.bfloat16)
    return result.reshape(row_count, column_count * block_size)


def local(inputs, weight_tiles, source_block, target_block, live_slots):
    section_pos = lax.axis_index("section")
    section_count = lax.axis_size("section")
    row_count, shard_width = inputs.shape
    slot_count = weight_tiles.shape[1]
    column_count = shard_width // weight_tiles.shape[2]
    source = source_block[0]
    live_mask = jnp.arange(slot_count, dtype=jnp.int32) < live_slots[0, 0]
    selector = (
        (target_block[0][:, None] == jnp.arange(column_count, dtype=jnp.int32)[None, :])
        & live_mask[:, None]
    ).astype(jnp.float32)

    def compute(gathered):
        return layer_apply(gathered, weight_tiles, source, selector)

    def empty(gathered):
        return jnp.zeros((row_count, shard_width), jnp.bfloat16)

    def step(step_num, current, collected, route):
        gathered = lax.all_gather(current, "neuron", axis=1, tiled=True)
        active = section_pos == step_num
        result = compute(gathered)
        collected = jnp.where(active, result, collected)
        if route is None:
            return (result, collected)
        return (lax.ppermute(result, "section", route), collected)

    collected = jnp.zeros((row_count, shard_width), jnp.bfloat16)
    current = inputs
    if UNROLL:
        for t in range(section_count - 1):
            current, collected = step(t, current, collected, [(t, t + 1)])
    else:
        route = [(i, i + 1) for i in range(section_count - 1)]
        current, collected = lax.fori_loop(
            0, section_count - 1, lambda t, c: step(t, c[0], c[1], route), (current, collected)
        )
    _, collected = step(section_count - 1, current, collected, None)
    return collected[None]


def solution(mesh):
    in_specs = (
        P(None, "neuron"),
        P("section", "neuron", None, None),
        P("section", "neuron"),
        P("section", "neuron"),
        P("section", "neuron"),
    )
    out_specs = P("section", None, "neuron")
    return jax.shard_map(local, mesh=mesh, in_specs=in_specs, out_specs=out_specs, check_vma=False)
```

profile of v0, /device:TPU:455, one launch (start us, length us, event | category | flops | bytes accessed | tf_op | source)
XLA Modules:
  0.0 809.9 jit_solution(16794483580277421957)
XLA Ops:
  0.7 19.8 %all_gather.96 = bf16[6,32768]{1,0:T(8,128)(2,1)S(1)} all-gather(bf16[6,2048]{1,0:T(8,128)(2,1)} %param.5), channel_id=1, replica_groups=mesh['section'=32,'neuron'=16] {'neuron'}, dimensions={1}, use_global_device_ids=true | all-gather | bytes 417792 | tf_op jit(solution)/shard_map/all_gather | solution.py:46
  47.7 16.8 %all_gather.98 = bf16[6,32768]{1,0:T(8,128)(2,1)S(1)} all-gather(bf16[6,2048]{1,0:T(8,128)(2,1)S(1)} %collective-permute-done.1), channel_id=1, replica_groups=mesh['section'=32,'neuron'=16] {'neuron'}, dimensions={1}, use_global_device_ids=true | all-gather | bytes 417792 | tf_op jit(solution)/shard_map/all_gather | solution.py:46
  91.2 16.8 %all_gather.100 = bf16[6,32768]{1,0:T(8,128)(2,1)S(1)} all-gather(bf16[6,2048]{1,0:T(8,128)(2,1)S(1)} %collective-permute-done.3), channel_id=1, replica_groups=mesh['section'=32,'neuron'=16] {'neuron'}, dimensions={1}, use_global_device_ids=true | all-gather | bytes 417792 | tf_op jit(solution)/shard_map/all_gather | solution.py:46
  134.7 16.8 %all_gather.102 = bf16[6,32768]{1,0:T(8,128)(2,1)S(1)} all-gather(bf16[6,2048]{1,0:T(8,128)(2,1)S(1)} %collective-permute-done.5), channel_id=1, replica_groups=mesh['section'=32,'neuron'=16] {'neuron'}, dimensions={1}, use_global_device_ids=true | all-gather | bytes 417792 | tf_op jit(solution)/shard_map/all_gather | solution.py:46
  178.2 17.2 %all_gather.104 = bf16[6,32768]{1,0:T(8,128)(2,1)S(1)} all-gather(bf16[6,2048]{1,0:T(8,128)(2,1)S(1)} %collective-permute-done.7), channel_id=1, replica_groups=mesh['section'=32,'neuron'=16] {'neuron'}, dimensions={1}, use_global_device_ids=true | all-gather | bytes 417792 | tf_op jit(solution)/shard_map/all_gather | solution.py:46
  222.2 16.8 %all_gather.106 = bf16[6,32768]{1,0:T(8,128)(2,1)S(1)} all-gather(bf16[6,2048]{1,0:T(8,128)(2,1)S(1)} %collective-permute-done.9), channel_id=1, replica_groups=mesh['section'=32,'neuron'=16] {'neuron'}, dimensions={1}, use_global_device_ids=true | all-gather | bytes 417792 | tf_op jit(solution)/shard_map/all_gather | solution.py:46
  265.7 16.8 %all_gather.108 = bf16[6,32768]{1,0:T(8,128)(2,1)S(1)} all-gather(bf16[6,2048]{1,0:T(8,128)(2,1)S(1)} %collective-permute-done.11), channel_id=1, replica_groups=mesh['section'=32,'neuron'=16] {'neuron'}, dimensions={1}, use_global_device_ids=true | all-gather | bytes 417792 | tf_op jit(solution)/shard_map/all_gather | solution.py:46
  309.2 16.7 %all_gather.110 = bf16[6,32768]{1,0:T(8,128)(2,1)S(1)} all-gather(bf16[6,2048]{1,0:T(8,128)(2,1)S(1)} %collective-permute-done.13), channel_id=1, replica_groups=mesh['section'=32,'neuron'=16] {'neuron'}, dimensions={1}, use_global_device_ids=true | all-gather | bytes 417792 | tf_op jit(solution)/shard_map/all_gather | solution.py:46
  352.6 16.9 %all_gather.112 = bf16[6,32768]{1,0:T(8,128)(2,1)S(1)} all-gather(bf16[6,2048]{1,0:T(8,128)(2,1)S(1)} %collective-permute-done.15), channel_id=1, replica_groups=mesh['section'=32,'neuron'=16] {'neuron'}, dimensions={1}, use_global_device_ids=true | all-gather | bytes 417792 | tf_op jit(solution)/shard_map/all_gather | solution.py:46
  396.1 16.7 %all_gather.114 = bf16[6,32768]{1,0:T(8,128)(2,1)S(1)} all-gather(bf16[6,2048]{1,0:T(8,128)(2,1)S(1)} %collective-permute-done.17), channel_id=1, replica_groups=mesh['section'=32,'neuron'=16] {'neuron'}, dimensions={1}, use_global_device_ids=true | all-gather | bytes 417792 | tf_op jit(solution)/shard_map/all_gather | solution.py:46
  417.9 16.4 %all_gather.115 = bf16[6,32768]{1,0:T(8,128)(2,1)S(1)} all-gather(bf16[6,2048]{1,0:T(8,128)(2,1)S(1)} %collective-permute-done.18), channel_id=1, replica_groups=mesh['section'=32,'neuron'=16] {'neuron'}, dimensions={1}, use_global_device_ids=true | all-gather | bytes 417792 | tf_op jit(solution)/shard_map/all_gather | solution.py:46
  439.3 16.7 %all_gather.116 = bf16[6,32768]{1,0:T(8,128)(2,1)S(1)} all-gather(bf16[6,2048]{1,0:T(8,128)(2,1)S(1)} %collective-permute-done.19), channel_id=1, replica_groups=mesh['section'=32,'neuron'=16] {'neuron'}, dimensions={1}, use_global_device_ids=true | all-gather | bytes 417792 | tf_op jit(solution)/shard_map/all_gather | solution.py:46
  461.1 16.4 %all_gather.117 = bf16[6,32768]{1,0:T(8,128)(2,1)S(1)} all-gather(bf16[6,2048]{1,0:T(8,128)(2,1)S(1)} %collective-permute-done.20), channel_id=1, replica_groups=mesh['section'=32,'neuron'=16] {'neuron'}, dimensions={1}, use_global_device_ids=true | all-gather | bytes 417792 | tf_op jit(solution)/shard_map/all_gather | solution.py:46
  482.6 16.7 %all_gather.118 = bf16[6,32768]{1,0:T(8,128)(2,1)S(1)} all-gather(bf16[6,2048]{1,0:T(8,128)(2,1)S(1)} %collective-permute-done.21), channel_id=1, replica_groups=mesh['section'=32,'neuron'=16] {'neuron'}, dimensions={1}, use_global_device_ids=true | all-gather | bytes 417792 | tf_op jit(solution)/shard_map/all_gather | solution.py:46
  504.4 16.4 %all_gather.119 = bf16[6,32768]{1,0:T(8,128)(2,1)S(1)} all-gather(bf16[6,2048]{1,0:T(8,128)(2,1)S(1)} %collective-permute-done.22), channel_id=1, replica_groups=mesh['section'=32,'neuron'=16] {'neuron'}, dimensions={1}, use_global_device_ids=true | all-gather | bytes 417792 | tf_op jit(solution)/shard_map/all_gather | solution.py:46
  525.9 16.9 %all_gather.120 = bf16[6,32768]{1,0:T(8,128)(2,1)S(1)} all-gather(bf16[6,2048]{1,0:T(8,128)(2,1)S(1)} %collective-permute-done.23), channel_id=1, replica_groups=mesh['section'=32,'neuron'=16] {'neuron'}, dimensions={1}, use_global_device_ids=true | all-gather | bytes 417792 | tf_op jit(solution)/shard_map/all_gather | solution.py:46
  547.8 16.4 %all_gather.121 = bf16[6,32768]{1,0:T(8,128)(2,1)S(1)} all-gather(bf16[6,2048]{1,0:T(8,128)(2,1)S(1)} %collective-permute-done.24), channel_id=1, replica_groups=mesh['section'=32,'neuron'=16] {'neuron'}, dimensions={1}, use_global_device_ids=true | all-gather | bytes 417792 | tf_op jit(solution)/shard_map/all_gather | solution.py:46
  569.3 16.7 %all_gather.122 = bf16[6,32768]{1,0:T(8,128)(2,1)S(1)} all-gather(bf16[6,2048]{1,0:T(8,128)(2,1)S(1)} %collective-permute-done.25), channel_id=1, replica_groups=mesh['section'=32,'neuron'=16] {'neuron'}, dimensions={1}, use_global_device_ids=true | all-gather | bytes 417792 | tf_op jit(solution)/shard_map/all_gather | solution.py:46
  591.1 16.4 %all_gather.123 = bf16[6,32768]{1,0:T(8,128)(2,1)S(1)} all-gather(bf16[6,2048]{1,0:T(8,128)(2,1)S(1)} %collective-permute-done.26), channel_id=1, replica_groups=mesh['section'=32,'neuron'=16] {'neuron'}, dimensions={1}, use_global_device_ids=true | all-gather | bytes 417792 | tf_op jit(solution)/shard_map/all_gather | solution.py:46
  612.6 16.7 %all_gather.124 = bf16[6,32768]{1,0:T(8,128)(2,1)S(1)} all-gather(bf16[6,2048]{1,0:T(8,128)(2,1)S(1)} %collective-permute-done.27), channel_id=1, replica_groups=mesh['section'=32,'neuron'=16] {'neuron'}, dimensions={1}, use_global_device_ids=true | all-gather | bytes 417792 | tf_op jit(solution)/shard_map/all_gather | solution.py:46
  634.3 16.5 %all_gather.125 = bf16[6,32768]{1,0:T(8,128)(2,1)S(1)} all-gather(bf16[6,2048]{1,0:T(8,128)(2,1)S(1)} %collective-permute-done.28), channel_id=1, replica_groups=mesh['section'=32,'neuron'=16] {'neuron'}, dimensions={1}, use_global_device_ids=true | all-gather | bytes 417792 | tf_op jit(solution)/shard_map/all_gather | solution.py:46
  655.9 16.7 %all_gather.126 = bf16[6,32768]{1,0:T(8,128)(2,1)S(1)} all-gather(bf16[6,2048]{1,0:T(8,128)(2,1)S(1)} %collective-permute-done.29), channel_id=1, replica_groups=mesh['section'=32,'neuron'=16] {'neuron'}, dimensions={1}, use_global_device_ids=true | all-gather | bytes 417792 | tf_op jit(solution)/shard_map/all_gather | solution.py:46
  679.2 107.5 %collective-permute-done.30 = bf16[6,2048]{1,0:T(8,128)(2,1)S(1)} collective-permute-done((bf16[6,2048]{1,0:T(8,128)(2,1)S(1)}, bf16[6,2048]{1,0:T(8,128)(2,1)S(1)}, u32[]{:S(2)}, u32[]{:S(2)}) %collective-permute-start.30) | collective-permute-done | bytes 24608 | tf_op jit(solution)/shard_map/ppermute | solution.py:52
  786.7 17.9 %all_gather.127 = bf16[6,32768]{1,0:T(8,128)(2,1)S(1)} all-gather(bf16[6,2048]{1,0:T(8,128)(2,1)S(1)} %collective-permute-done.30), channel_id=1, replica_groups=mesh['section'=32,'neuron'=16] {'neuron'}, dimensions={1}, use_global_device_ids=true | all-gather | bytes 417792 | tf_op jit(solution)/shard_map/all_gather | solution.py:46
  (224 shorter events, 312.4 us)
Async XLA Ops:
  25.5 0.7 collective-permute-start
  47.0 0.7 collective-permute-start.1
  69.0 0.7 collective-permute-start.2
  90.5 0.7 collective-permute-start.3
  112.5 0.7 collective-permute-start.4
  134.1 0.7 collective-permute-start.5
  156.0 0.7 collective-permute-start.6
  177.6 0.7 collective-permute-start.7
  200.0 0.7 collective-permute-start.8
  221.5 0.7 collective-permute-start.9
  243.5 0.7 collective-permute-start.10
  265.0 0.7 collective-permute-start.11
  330.5 0.7 collective-permute-start.14
  395.4 0.7 collective-permute-start.17
  438.7 0.7 collective-permute-start.19
  460.4 0.7 collective-permute-start.20
  481.9 0.7 collective-permute-start.21
  503.7 0.7 collective-permute-start.22
  525.2 0.7 collective-permute-start.23
  547.2 0.7 collective-permute-start.24
  590.4 0.7 collective-permute-start.26
  611.9 0.7 collective-permute-start.27
  655.2 0.7 collective-permute-start.29
  676.9 109.8 %collective-permute-start.30 = (bf16[6,2048]{1,0:T(8,128)(2,1)S(1)}, bf16[6,2048]{1,0:T(8,128)(2,1)S(1)}, u32[]{:S(2)}, u32[]{:S(2)}) collective-permute-start(bf16[6,2048]{1,0:T(8,128)(2,1)S(1)} %bitcast.647), channel_id=1, source_target_pairs={{480,496},{481,497},{482,498},{483,499},{484,500},{485,501},{486,5... | collective-permute-start | bytes 73736 | tf_op jit(solution)/shard_map/ppermute | solution.py:52
  (10 other events, 111.1 us)
where the time goes:
time: 820 us; the launch traced here: 810 us
  blocking collectives  536 us (65%)
  matrix products  117 us (14%)
  waiting for transfers between devices  108 us (13%)
  local copies, waits for them, and re-layouts  25.1 us (3%)
  starting transfers between devices  21.2 us (3%)
    all_gather x32, blocking collectives, step(): gathered = lax.all_gather(current, 'neuron', axis=1, tiled=True)  536 us
    dot_general x32, matrix products, layer_apply(): jnp.einsum('msk,skj->msj', picked, weight_tiles[0], preferred_element_typ...  108 us
    ppermute x31, waiting for transfers between devices, step(): return (lax.ppermute(result, 'section', route), collected)  108 us
    gather x32, local copies, waits for them, and re-layouts, layer_apply(): picked = shaped.at[:, source].get(mode='promise_in_bounds')  23.9 us
    ppermute x31, starting transfers between devices, step(): return (lax.ppermute(result, 'section', route), collected)  21.2 us
  transfers between devices with their start and end apart: 31, of which 1 were waited for; matrix products, arithmetic and copies ran while one was open for 0% of the time, Pallas kernels for 0%

commit v1 on v0

--- a/solution.py
+++ b/solution.py
@@ -6,6 +6,28 @@
 NEURON_BIAS = -0.3
 CLIP_LEVEL = 32.0
 UNROLL = True
+
+
+def joined_along(parts, dim):
+    shape = list(parts.shape[1:])
+    shape[dim] *= parts.shape[0]
+    return jnp.moveaxis(parts, 0, dim).reshape(shape)
+
+
+def collect(x, axis, dim):
+    size = lax.axis_size(axis)
+    pairs = [(i, (i + 1) % size) for i in range(size)]
+    back = [(b, a) for a, b in pairs]
+    lower, upper = ([], [])
+    for turn in range(size - 1):
+        if turn % 2 == 0:
+            lower.append(lax.ppermute(lower[-1] if lower else x, axis, pairs))
+        else:
+            upper.append(lax.ppermute(upper[-1] if upper else x, axis, back))
+    blocks = jnp.stack([*lower[::-1], x, *upper])
+    shift = lax.axis_index(axis) - len(lower)
+    blocks = blocks[(jnp.arange(size) - shift) % size]
+    return joined_along(blocks, dim)
 
 
 def layer_apply(gathered, weight_tiles, source, selector):
@@ -43,7 +65,7 @@
         return jnp.zeros((row_count, shard_width), jnp.bfloat16)
 
     def step(step_num, current, collected, route):
-        gathered = lax.all_gather(current, "neuron", axis=1, tiled=True)
+        gathered = collect(current, "neuron", 1)
         active = section_pos == step_num
         result = compute(gathered)
         collected = jnp.where(active, result, collected)

time: 820 us -> 1800 us (2.20)
  the two profiles are of different devices: /device:TPU:455 before, /device:TPU:511 now
where the time goes in v1:
time: 1800 us; the launch traced here: 1790 us
  starting transfers between devices  916 us (51%)
  waiting for transfers between devices  382 us (21%)
  local copies, waits for them, and re-layouts  366 us (20%)
  matrix products  117 us (6%)
    ppermute x256, starting transfers between devices, collect(): lower.append(lax.ppermute(lower[-1] if lower else x, axis, pairs))  893 us
    unnamed x517, local copies, waits for them, and re-layouts  268 us
    ppermute x256, waiting for transfers between devices, collect(): lower.append(lax.ppermute(lower[-1] if lower else x, axis, pairs))  257 us
    ppermute x31, waiting for transfers between devices, step(): return (lax.ppermute(result, 'section', route), collected)  111 us
    dot_general x32, matrix products, layer_apply(): jnp.einsum('msk,skj->msj', picked, weight_tiles[0], preferred_element_typ...  108 us
    gather x32, local copies, waits for them, and re-layouts, collect(): blocks = blocks[(jnp.arange(size) - shift) % size]  52.5 us
  transfers between devices with their start and end apart: 511, of which 264 were waited for; matrix products, arithmetic and copies ran while one was open for 15% of the time, Pallas kernels for 0%

profile of v1, /device:TPU:511, one launch (start us, length us, event | category | flops | bytes accessed | tf_op | source)
XLA Modules:
  0.0 1785.1 jit_solution(14044597562548292330)
XLA Ops:
  92.9 3.5 collective-permute-start.32
  146.1 3.5 collective-permute-start.48
  199.3 3.5 collective-permute-start.64
  305.8 3.5 collective-permute-start.96
  412.2 3.5 collective-permute-start.128
  465.4 3.5 collective-permute-start.144
  571.8 3.5 collective-permute-start.176
  625.0 3.5 collective-permute-start.192
  678.4 3.5 collective-permute-start.208
  731.6 3.5 collective-permute-start.224
  784.8 3.5 collective-permute-start.240
  880.4 3.5 collective-permute-start.272
  933.6 3.5 collective-permute-start.288
  987.2 3.5 collective-permute-start.304
  1040.4 3.5 collective-permute-start.320
  1093.6 3.5 collective-permute-start.336
  1146.8 3.5 collective-permute-start.352
  1200.0 3.5 collective-permute-start.368
  1253.2 3.5 collective-permute-start.384
  1306.4 3.5 collective-permute-start.400
  1359.7 3.5 collective-permute-start.416
  1626.3 111.2 %collective-permute-done.495 = bf16[6,2048]{1,0:T(8,128)(2,1)S(1)} collective-permute-done((bf16[6,2048]{1,0:T(8,128)(2,1)S(1)}, bf16[6,2048]{1,0:T(8,128)(2,1)S(1)}, u32[]{:S(2)}, u32[]{:S(2)}) %collective-permute-start.495) | collective-permute-done | bytes 24608 | tf_op jit(solution)/shard_map/ppermute | solution.py:74
  1737.5 4.1 collective-permute-start.496
  1774.7 4.3 collective-permute-done.510
  (1698 shorter events, 1588.2 us)
Async XLA Ops:
  75.1 10.2 collective-permute-start.30
  128.3 10.2 collective-permute-start.46
  181.5 10.2 collective-permute-start.62
  234.7 10.2 collective-permute-start.78
  287.9 10.2 collective-permute-start.94
  341.2 10.2 collective-permute-start.110
  394.4 10.2 collective-permute-start.126
  447.6 10.2 collective-permute-start.142
  500.8 10.2 collective-permute-start.158
  554.0 10.2 collective-permute-start.174
  607.2 10.2 collective-permute-start.190
  660.4 10.2 collective-permute-start.206
  713.8 10.2 collective-permute-start.222
  767.0 10.2 collective-permute-start.238
  862.7 10.2 collective-permute-start.270
  915.8 10.2 collective-permute-start.286
  969.0 10.2 collective-permute-start.302
  1022.6 10.2 collective-permute-start.318
  1075.8 10.2 collective-permute-start.334
  1129.0 10.2 collective-permute-start.350
  1182.2 10.2 collective-permute-start.366
  1235.4 10.2 collective-permute-start.382
  1501.5 10.2 collective-permute-start.462
  1625.0 112.5 %collective-permute-start.495 = (bf16[6,2048]{1,0:T(8,128)(2,1)S(1)}, bf16[6,2048]{1,0:T(8,128)(2,1)S(1)}, u32[]{:S(2)}, u32[]{:S(2)}) collective-permute-start(bf16[6,2048]{1,0:T(8,128)(2,1)S(1)} %bitcast.1797), channel_id=1, source_target_pairs={{480,496},{481,497},{482,498},{483,499},{484,500},{485,501},{486,5... | collective-permute-start | bytes 73736 | tf_op jit(solution)/shard_map/ppermute | solution.py:74
  (490 other events, 2279.9 us)
